TPU v7x, 512 devices: a whole 4x4x16 slice. The times are simulated.
512 devices in a mesh: pipe: 16 (over z), seq: 8 (over y, core), dp: 4 (over x).
Axes of the slice: x: 4, y: 4, z: 16, core: 2. Of those that a mesh axis runs over, the one named last changes fastest.
Arguments:
- acts: bfloat16 [16, 4, 1024, 8192], P('pipe', 'dp', 'seq'), may hold values from -6 to 6
- top_grad: bfloat16 [4, 1024, 8192], P('dp', 'seq'), may hold values from -6 to 6
- a_rows: bfloat16 [16, 32, 8192], P('pipe', None, ('seq', 'dp')), may hold values from -1 to 1
- b_rows: bfloat16 [16, 32, 8192], P('pipe', None, ('seq', 'dp')), may hold values from -0.375 to 0.375
- gain: bfloat16 [16, 8192], P('pipe', ('seq', 'dp')), may hold values from 0.5 to 1.5
Outputs:
- grad_a: float32 [16, 32, 8192], P('pipe', None, ('seq', 'dp'))
- grad_b: float32 [16, 32, 8192], P('pipe', None, ('seq', 'dp'))
- grad_gain: float32 [16, 8192], P('pipe', ('seq', 'dp'))
- clip_factors: float32 [4], P('dp')
All inputs are finite; a program needn't handle non-finite values.
Results may differ from a plain program's by a relative error of at most 0.019.
Values may be sent and summed in bfloat16 or wider, within the bound.
No kernel may reach another device: no remote copies, remote signals or barrier semaphores. Data moves between devices by JAX's collectives and lax.ppermute only.
A program may use at most 64 MiB of HBM per device.

v0:
```python
import math
import jax
import jax.numpy as jnp
from jax import lax
from jax.sharding import PartitionSpec as P

rows_per_block = 16


def from_behind(value, axis, steps):
    count = lax.axis_size(axis)
    initial, last = (max(0, -steps), min(count, count - steps))
    return lax.ppermute(value, axis, [(source, source + steps) for source in range(initial, last)])


def on_device(acts, top_grad, a_rows, b_rows, gain):
    sections = lax.axis_size("pipe")
    section = lax.axis_index("pipe")
    hidden = acts[0, 0]
    top = top_grad[0]
    rank = a_rows.shape[1]
    params = jnp.concatenate([a_rows[0], b_rows[0], gain], axis=0)
    whole = lax.all_gather(params, ("seq", "dp"), axis=1, tiled=True)
    a_full = whole[:rank]
    b_full = whole[rank : 2 * rank]
    gain_float = whole[2 * rank].astype(jnp.float32)
    rows, width = hidden.shape
    block_total = rows // rows_per_block
    hidden_float = hidden.astype(jnp.float32)
    inverse_root_mean = jnp.sqrt(
        jnp.mean(hidden_float * hidden_float, axis=-1, keepdims=True) + 1e-05
    )
    input_normalized = hidden_float / inverse_root_mean
    normalized_rows = (input_normalized * gain_float).astype(jnp.bfloat16)
    low = jnp.dot(normalized_rows, a_full.T, preferred_element_type=jnp.float32).astype(
        jnp.bfloat16
    )
    contract_last = (((1,), (1,)), ((), ()))
    contract_first = (((0,), (0,)), ((), ()))

    def back_block(upstream_gradient, block_offset):
        hidden_part = lax.dynamic_slice_in_dim(hidden, block_offset, rows_per_block, 0)
        r_part = lax.dynamic_slice_in_dim(inverse_root_mean, block_offset, rows_per_block, 0)
        input_portion = hidden_part.astype(jnp.float32) / r_part
        d_low = lax.dot_general(
            upstream_gradient, b_full, contract_last, preferred_element_type=jnp.float32
        ).astype(jnp.bfloat16)
        normalized_gradient = jnp.dot(d_low, a_full, preferred_element_type=jnp.float32)
        input_gradient = normalized_gradient * gain_float
        hidden_gradient = (
            upstream_gradient.astype(jnp.float32)
            + (
                input_gradient
                - input_portion * jnp.mean(input_gradient * input_portion, axis=-1, keepdims=True)
            )
            / r_part
        )
        return hidden_gradient.astype(jnp.bfloat16)

    def turn(turn_index, carry):
        incoming, store = carry
        block_index = turn_index - (sections - 1 - section)
        inside = jnp.logical_and(block_index >= 0, block_index < block_total)
        block_offset = jnp.clip(block_index, 0, block_total - 1) * rows_per_block
        top_block = lax.dynamic_slice_in_dim(top, block_offset, rows_per_block, 0)
        source = jnp.where(section == sections - 1, top_block, incoming)
        slot = jnp.where(inside, block_index, block_total)
        store = lax.dynamic_update_slice_in_dim(store, source[None], slot, 0)
        result = back_block(source, block_offset)
        incoming = from_behind(result, "pipe", -1)
        return (incoming, store)

    begin = (
        jnp.zeros((rows_per_block, width), jnp.bfloat16),
        jnp.zeros((block_total + 1, rows_per_block, width), jnp.bfloat16),
    )
    store = lax.fori_loop(0, sections + block_total - 1, turn, begin)[1]
    mine = store[:block_total].reshape(rows, width)
    d_low = lax.dot_general(mine, b_full, contract_last, preferred_element_type=jnp.float32).astype(
        jnp.bfloat16
    )
    normalized_gradient = jnp.dot(d_low, a_full, preferred_element_type=jnp.float32)
    grad_a = lax.dot_general(
        d_low, normalized_rows, contract_first, preferred_element_type=jnp.float32
    )
    grad_b = lax.dot_general(low, mine, contract_first, preferred_element_type=jnp.float32)
    gain_gradient = jnp.sum(normalized_gradient * input_normalized, axis=0)[None, :]
    grads = jnp.concatenate([grad_a, grad_b, gain_gradient], axis=0)
    part = lax.psum_scatter(grads, "seq", scatter_dimension=1, tiled=True)
    examples = lax.axis_size("dp")
    example = lax.axis_index("dp")
    square = jnp.sum(part * part)
    squares = jnp.where(jnp.arange(examples) == example, square, 0.0).astype(jnp.float32)
    totals = lax.psum(squares, ("pipe", "seq", "dp"))
    bound = math.sqrt(sections * (2 * rank + 1) * width)
    factors = bound / (jnp.sqrt(totals) + 0.01 * bound)
    gathered = lax.all_gather(part, "dp", axis=0, tiled=False)
    share = part.shape[1] // examples
    pieces = lax.dynamic_slice_in_dim(gathered, example * share, share, 2)
    combined = jnp.sum(factors[:, None, None] * pieces, axis=0)
    out_a = combined[:rank]
    out_b = combined[rank : 2 * rank]
    out_g = combined[2 * rank :]
    factor = lax.dynamic_slice_in_dim(factors, example, 1, 0)
    return (out_a[None], out_b[None], out_g, factor)


def solution(mesh):
    in_specs = (
        P("pipe", "dp", "seq", None),
        P("dp", "seq", None),
        P("pipe", None, ("seq", "dp")),
        P("pipe", None, ("seq", "dp")),
        P("pipe", ("seq", "dp")),
    )
    out_specs = (
        P("pipe", None, ("seq", "dp")),
        P("pipe", None, ("seq", "dp")),
        P("pipe", ("seq", "dp")),
        P("dp"),
    )
    return jax.shard_map(
        on_device, mesh=mesh, in_specs=in_specs, out_specs=out_specs, check_vma=False
    )
```

profile of v0, /device:TPU:1, one launch (start us, length us, event | category | flops | bytes accessed | tf_op | source)
XLA Modules:
  0.0 594.1 jit_solution(15978239011922078406)
XLA Ops:
  10.8 64.3 %all-gather.5.cloned.1.call-done = bf16[65,8192]{1,0:T(8,128)(2,1)} async-done(((bf16[65,256]{1,0:T(8,128)(2,1)}), bf16[65,8192]{1,0:T(8,128)(2,1)}) %all-gather.5.cloned.1.call-update) | async-done | bytes 1064976 | tf_op jit(solution)/shard_map/all_gather | solution.py:23
  78.5 318.4 %while.17 = (s32[]{:T(128)}, bf16[16,8192]{1,0:T(8,128)(2,1)S(1)}, bf16[9,16,8192]{2,1,0:T(8,128)(2,1)S(1)}, pred[]{:T(512)}, s32[]{:T(128)}, /*index=5*/bf16[12...) while((s32[]{:T(128)}, bf16[16,8192]{1,0:T(8,128)(2,1)S(1)}, ...), condition=%wide.region_3.4_spmd, body=%wide.region_1.3_spmd.sunk | while | flops 18612752 | bytes 5538680 | solution.py:77
  84.7 8.4 %collective-permute-done = bf16[16,8192]{1,0:T(8,128)(2,1)S(1)} collective-permute-done((bf16[16,8192]{1,0:T(8,128)(2,1)}, bf16[16,8192]{1,0:T(8,128)(2,1)S(1)}, u32[]{:S(2)}, u32[]{:S(2)}) %collective-permute-start) | collective-permute-done | bytes 262176 | tf_op jit(solution)/shard_map/while/body/eval_jaxpr/ppermute | solution.py:13
  99.3 7.5 %collective-permute-done = bf16[16,8192]{1,0:T(8,128)(2,1)S(1)} collective-permute-done((bf16[16,8192]{1,0:T(8,128)(2,1)}, bf16[16,8192]{1,0:T(8,128)(2,1)S(1)}, u32[]{:S(2)}, u32[]{:S(2)}) %collective-permute-start) | collective-permute-done | bytes 262176 | tf_op jit(solution)/shard_map/while/body/eval_jaxpr/ppermute | solution.py:13
  113.0 6.7 %collective-permute-done = bf16[16,8192]{1,0:T(8,128)(2,1)S(1)} collective-permute-done((bf16[16,8192]{1,0:T(8,128)(2,1)}, bf16[16,8192]{1,0:T(8,128)(2,1)S(1)}, u32[]{:S(2)}, u32[]{:S(2)}) %collective-permute-start) | collective-permute-done | bytes 262176 | tf_op jit(solution)/shard_map/while/body/eval_jaxpr/ppermute | solution.py:13
  125.9 8.2 %collective-permute-done = bf16[16,8192]{1,0:T(8,128)(2,1)S(1)} collective-permute-done((bf16[16,8192]{1,0:T(8,128)(2,1)}, bf16[16,8192]{1,0:T(8,128)(2,1)S(1)}, u32[]{:S(2)}, u32[]{:S(2)}) %collective-permute-start) | collective-permute-done | bytes 262176 | tf_op jit(solution)/shard_map/while/body/eval_jaxpr/ppermute | solution.py:13
  165.7 7.2 %collective-permute-done = bf16[16,8192]{1,0:T(8,128)(2,1)S(1)} collective-permute-done((bf16[16,8192]{1,0:T(8,128)(2,1)}, bf16[16,8192]{1,0:T(8,128)(2,1)S(1)}, u32[]{:S(2)}, u32[]{:S(2)}) %collective-permute-start) | collective-permute-done | bytes 262176 | tf_op jit(solution)/shard_map/while/body/eval_jaxpr/ppermute | solution.py:13
  179.1 7.2 %collective-permute-done = bf16[16,8192]{1,0:T(8,128)(2,1)S(1)} collective-permute-done((bf16[16,8192]{1,0:T(8,128)(2,1)}, bf16[16,8192]{1,0:T(8,128)(2,1)S(1)}, u32[]{:S(2)}, u32[]{:S(2)}) %collective-permute-start) | collective-permute-done | bytes 262176 | tf_op jit(solution)/shard_map/while/body/eval_jaxpr/ppermute | solution.py:13
  192.5 7.2 %collective-permute-done = bf16[16,8192]{1,0:T(8,128)(2,1)S(1)} collective-permute-done((bf16[16,8192]{1,0:T(8,128)(2,1)}, bf16[16,8192]{1,0:T(8,128)(2,1)S(1)}, u32[]{:S(2)}, u32[]{:S(2)}) %collective-permute-start) | collective-permute-done | bytes 262176 | tf_op jit(solution)/shard_map/while/body/eval_jaxpr/ppermute | solution.py:13
  206.0 7.2 %collective-permute-done = bf16[16,8192]{1,0:T(8,128)(2,1)S(1)} collective-permute-done((bf16[16,8192]{1,0:T(8,128)(2,1)}, bf16[16,8192]{1,0:T(8,128)(2,1)S(1)}, u32[]{:S(2)}, u32[]{:S(2)}) %collective-permute-start) | collective-permute-done | bytes 262176 | tf_op jit(solution)/shard_map/while/body/eval_jaxpr/ppermute | solution.py:13
  219.4 7.2 %collective-permute-done = bf16[16,8192]{1,0:T(8,128)(2,1)S(1)} collective-permute-done((bf16[16,8192]{1,0:T(8,128)(2,1)}, bf16[16,8192]{1,0:T(8,128)(2,1)S(1)}, u32[]{:S(2)}, u32[]{:S(2)}) %collective-permute-start) | collective-permute-done | bytes 262176 | tf_op jit(solution)/shard_map/while/body/eval_jaxpr/ppermute | solution.py:13
  232.8 7.2 %collective-permute-done = bf16[16,8192]{1,0:T(8,128)(2,1)S(1)} collective-permute-done((bf16[16,8192]{1,0:T(8,128)(2,1)}, bf16[16,8192]{1,0:T(8,128)(2,1)S(1)}, u32[]{:S(2)}, u32[]{:S(2)}) %collective-permute-start) | collective-permute-done | bytes 262176 | tf_op jit(solution)/shard_map/while/body/eval_jaxpr/ppermute | solution.py:13
  246.3 8.4 %collective-permute-done = bf16[16,8192]{1,0:T(8,128)(2,1)S(1)} collective-permute-done((bf16[16,8192]{1,0:T(8,128)(2,1)}, bf16[16,8192]{1,0:T(8,128)(2,1)S(1)}, u32[]{:S(2)}, u32[]{:S(2)}) %collective-permute-start) | collective-permute-done | bytes 262176 | tf_op jit(solution)/shard_map/while/body/eval_jaxpr/ppermute | solution.py:13
  260.9 10.0 %collective-permute-done = bf16[16,8192]{1,0:T(8,128)(2,1)S(1)} collective-permute-done((bf16[16,8192]{1,0:T(8,128)(2,1)}, bf16[16,8192]{1,0:T(8,128)(2,1)S(1)}, u32[]{:S(2)}, u32[]{:S(2)}) %collective-permute-start) | collective-permute-done | bytes 262176 | tf_op jit(solution)/shard_map/while/body/eval_jaxpr/ppermute | solution.py:13
  277.1 10.7 %collective-permute-done = bf16[16,8192]{1,0:T(8,128)(2,1)S(1)} collective-permute-done((bf16[16,8192]{1,0:T(8,128)(2,1)}, bf16[16,8192]{1,0:T(8,128)(2,1)S(1)}, u32[]{:S(2)}, u32[]{:S(2)}) %collective-permute-start) | collective-permute-done | bytes 262176 | tf_op jit(solution)/shard_map/while/body/eval_jaxpr/ppermute | solution.py:13
  294.0 9.9 %collective-permute-done = bf16[16,8192]{1,0:T(8,128)(2,1)S(1)} collective-permute-done((bf16[16,8192]{1,0:T(8,128)(2,1)}, bf16[16,8192]{1,0:T(8,128)(2,1)S(1)}, u32[]{:S(2)}, u32[]{:S(2)}) %collective-permute-start) | collective-permute-done | bytes 262176 | tf_op jit(solution)/shard_map/while/body/eval_jaxpr/ppermute | solution.py:13
  310.1 7.9 %collective-permute-done = bf16[16,8192]{1,0:T(8,128)(2,1)S(1)} collective-permute-done((bf16[16,8192]{1,0:T(8,128)(2,1)}, bf16[16,8192]{1,0:T(8,128)(2,1)S(1)}, u32[]{:S(2)}, u32[]{:S(2)}) %collective-permute-start) | collective-permute-done | bytes 262176 | tf_op jit(solution)/shard_map/while/body/eval_jaxpr/ppermute | solution.py:13
  324.2 6.7 %collective-permute-done = bf16[16,8192]{1,0:T(8,128)(2,1)S(1)} collective-permute-done((bf16[16,8192]{1,0:T(8,128)(2,1)}, bf16[16,8192]{1,0:T(8,128)(2,1)S(1)}, u32[]{:S(2)}, u32[]{:S(2)}) %collective-permute-start) | collective-permute-done | bytes 262176 | tf_op jit(solution)/shard_map/while/body/eval_jaxpr/ppermute | solution.py:13
  349.6 7.0 %collective-permute-done = bf16[16,8192]{1,0:T(8,128)(2,1)S(1)} collective-permute-done((bf16[16,8192]{1,0:T(8,128)(2,1)}, bf16[16,8192]{1,0:T(8,128)(2,1)S(1)}, u32[]{:S(2)}, u32[]{:S(2)}) %collective-permute-start) | collective-permute-done | bytes 262176 | tf_op jit(solution)/shard_map/while/body/eval_jaxpr/ppermute | solution.py:13
  362.8 7.2 %collective-permute-done = bf16[16,8192]{1,0:T(8,128)(2,1)S(1)} collective-permute-done((bf16[16,8192]{1,0:T(8,128)(2,1)}, bf16[16,8192]{1,0:T(8,128)(2,1)S(1)}, u32[]{:S(2)}, u32[]{:S(2)}) %collective-permute-start) | collective-permute-done | bytes 262176 | tf_op jit(solution)/shard_map/while/body/eval_jaxpr/ppermute | solution.py:13
  376.2 7.2 %collective-permute-done = bf16[16,8192]{1,0:T(8,128)(2,1)S(1)} collective-permute-done((bf16[16,8192]{1,0:T(8,128)(2,1)}, bf16[16,8192]{1,0:T(8,128)(2,1)S(1)}, u32[]{:S(2)}, u32[]{:S(2)}) %collective-permute-start) | collective-permute-done | bytes 262176 | tf_op jit(solution)/shard_map/while/body/eval_jaxpr/ppermute | solution.py:13
  389.7 7.2 %collective-permute-done = bf16[16,8192]{1,0:T(8,128)(2,1)S(1)} collective-permute-done((bf16[16,8192]{1,0:T(8,128)(2,1)}, bf16[16,8192]{1,0:T(8,128)(2,1)S(1)}, u32[]{:S(2)}, u32[]{:S(2)}) %collective-permute-start) | collective-permute-done | bytes 262176 | tf_op jit(solution)/shard_map/while/body/eval_jaxpr/ppermute | solution.py:13
  410.6 65.9 %reduce-scatter.2.cloned.1.call-done = f32[65,1024]{1,0:T(8,128)} async-done(((f32[65,8192]{1,0:T(8,128)}), f32[65,1024]{1,0:T(8,128)}) %reduce-scatter.2.cloned.1.call-update) | async-done | bytes 266256 | tf_op jit(solution)/shard_map/reduce_scatter | solution.py:89
  478.8 106.0 %psum.7 = f32[4]{0:T(128)S(1)} all-reduce(f32[4]{0:T(128)S(1)} %compare_select_fusion), channel_id=1, replica_groups=mesh['pipe'=16,'seq'=8,'dp'=4] {'pipe','seq','dp'}, use_global_device_ids=true, to_apply=%region_7.8 | all-reduce | flops 4 | bytes 32 | tf_op jit(solution)/shard_map/psum | solution.py:94
  (184 shorter events, 187.3 us)
Async XLA Ops:
  7.2 67.9 %all-gather.5.cloned.1.call-start = ((), (), s32[]{:S(2)}) async-start(), calls=%async_computation.1 | async-start | bytes 1216512 | tf_op jit(solution)/shard_map/all_gather | solution.py:23
  8.6 467.8 %reduce-scatter.2.cloned.1.call-start = ((), (), s32[]{:S(2)}) async-start(), calls=%async_computation.2 | async-start | bytes 2654208 | tf_op jit(solution)/shard_map/reduce_scatter | solution.py:89
  83.4 9.7 %collective-permute-start = (bf16[16,8192]{1,0:T(8,128)(2,1)}, bf16[16,8192]{1,0:T(8,128)(2,1)S(1)}, u32[]{:S(2)}, u32[]{:S(2)}) collective-permute-start(bf16[16,8192]{1,0:T(8,128)(2,1)} %add_convert_fusion.2), channel_id=1, source_target_pairs={{32,0},{64,32},{96,64},{128,96},{160,128},{192,160},{224,192},{256... | collective-permute-start | bytes 786440 | tf_op jit(solution)/shard_map/while/body/eval_jaxpr/ppermute | solution.py:13
  98.0 8.8 %collective-permute-start = (bf16[16,8192]{1,0:T(8,128)(2,1)}, bf16[16,8192]{1,0:T(8,128)(2,1)S(1)}, u32[]{:S(2)}, u32[]{:S(2)}) collective-permute-start(bf16[16,8192]{1,0:T(8,128)(2,1)} %add_convert_fusion.2), channel_id=1, source_target_pairs={{32,0},{64,32},{96,64},{128,96},{160,128},{192,160},{224,192},{256... | collective-permute-start | bytes 786440 | tf_op jit(solution)/shard_map/while/body/eval_jaxpr/ppermute | solution.py:13
  111.7 8.0 %collective-permute-start = (bf16[16,8192]{1,0:T(8,128)(2,1)}, bf16[16,8192]{1,0:T(8,128)(2,1)S(1)}, u32[]{:S(2)}, u32[]{:S(2)}) collective-permute-start(bf16[16,8192]{1,0:T(8,128)(2,1)} %add_convert_fusion.2), channel_id=1, source_target_pairs={{32,0},{64,32},{96,64},{128,96},{160,128},{192,160},{224,192},{256... | collective-permute-start | bytes 786440 | tf_op jit(solution)/shard_map/while/body/eval_jaxpr/ppermute | solution.py:13
  124.6 9.5 %collective-permute-start = (bf16[16,8192]{1,0:T(8,128)(2,1)}, bf16[16,8192]{1,0:T(8,128)(2,1)S(1)}, u32[]{:S(2)}, u32[]{:S(2)}) collective-permute-start(bf16[16,8192]{1,0:T(8,128)(2,1)} %add_convert_fusion.2), channel_id=1, source_target_pairs={{32,0},{64,32},{96,64},{128,96},{160,128},{192,160},{224,192},{256... | collective-permute-start | bytes 786440 | tf_op jit(solution)/shard_map/while/body/eval_jaxpr/ppermute | solution.py:13
  151.6 7.9 %collective-permute-start = (bf16[16,8192]{1,0:T(8,128)(2,1)}, bf16[16,8192]{1,0:T(8,128)(2,1)S(1)}, u32[]{:S(2)}, u32[]{:S(2)}) collective-permute-start(bf16[16,8192]{1,0:T(8,128)(2,1)} %add_convert_fusion.2), channel_id=1, source_target_pairs={{32,0},{64,32},{96,64},{128,96},{160,128},{192,160},{224,192},{256... | collective-permute-start | bytes 786440 | tf_op jit(solution)/shard_map/while/body/eval_jaxpr/ppermute | solution.py:13
  164.4 8.5 %collective-permute-start = (bf16[16,8192]{1,0:T(8,128)(2,1)}, bf16[16,8192]{1,0:T(8,128)(2,1)S(1)}, u32[]{:S(2)}, u32[]{:S(2)}) collective-permute-start(bf16[16,8192]{1,0:T(8,128)(2,1)} %add_convert_fusion.2), channel_id=1, source_target_pairs={{32,0},{64,32},{96,64},{128,96},{160,128},{192,160},{224,192},{256... | collective-permute-start | bytes 786440 | tf_op jit(solution)/shard_map/while/body/eval_jaxpr/ppermute | solution.py:13
  177.8 8.5 %collective-permute-start = (bf16[16,8192]{1,0:T(8,128)(2,1)}, bf16[16,8192]{1,0:T(8,128)(2,1)S(1)}, u32[]{:S(2)}, u32[]{:S(2)}) collective-permute-start(bf16[16,8192]{1,0:T(8,128)(2,1)} %add_convert_fusion.2), channel_id=1, source_target_pairs={{32,0},{64,32},{96,64},{128,96},{160,128},{192,160},{224,192},{256... | collective-permute-start | bytes 786440 | tf_op jit(solution)/shard_map/while/body/eval_jaxpr/ppermute | solution.py:13
  191.2 8.5 %collective-permute-start = (bf16[16,8192]{1,0:T(8,128)(2,1)}, bf16[16,8192]{1,0:T(8,128)(2,1)S(1)}, u32[]{:S(2)}, u32[]{:S(2)}) collective-permute-start(bf16[16,8192]{1,0:T(8,128)(2,1)} %add_convert_fusion.2), channel_id=1, source_target_pairs={{32,0},{64,32},{96,64},{128,96},{160,128},{192,160},{224,192},{256... | collective-permute-start | bytes 786440 | tf_op jit(solution)/shard_map/while/body/eval_jaxpr/ppermute | solution.py:13
  204.7 8.5 %collective-permute-start = (bf16[16,8192]{1,0:T(8,128)(2,1)}, bf16[16,8192]{1,0:T(8,128)(2,1)S(1)}, u32[]{:S(2)}, u32[]{:S(2)}) collective-permute-start(bf16[16,8192]{1,0:T(8,128)(2,1)} %add_convert_fusion.2), channel_id=1, source_target_pairs={{32,0},{64,32},{96,64},{128,96},{160,128},{192,160},{224,192},{256... | collective-permute-start | bytes 786440 | tf_op jit(solution)/shard_map/while/body/eval_jaxpr/ppermute | solution.py:13
  218.1 8.5 %collective-permute-start = (bf16[16,8192]{1,0:T(8,128)(2,1)}, bf16[16,8192]{1,0:T(8,128)(2,1)S(1)}, u32[]{:S(2)}, u32[]{:S(2)}) collective-permute-start(bf16[16,8192]{1,0:T(8,128)(2,1)} %add_convert_fusion.2), channel_id=1, source_target_pairs={{32,0},{64,32},{96,64},{128,96},{160,128},{192,160},{224,192},{256... | collective-permute-start | bytes 786440 | tf_op jit(solution)/shard_map/while/body/eval_jaxpr/ppermute | solution.py:13
  231.6 8.5 %collective-permute-start = (bf16[16,8192]{1,0:T(8,128)(2,1)}, bf16[16,8192]{1,0:T(8,128)(2,1)S(1)}, u32[]{:S(2)}, u32[]{:S(2)}) collective-permute-start(bf16[16,8192]{1,0:T(8,128)(2,1)} %add_convert_fusion.2), channel_id=1, source_target_pairs={{32,0},{64,32},{96,64},{128,96},{160,128},{192,160},{224,192},{256... | collective-permute-start | bytes 786440 | tf_op jit(solution)/shard_map/while/body/eval_jaxpr/ppermute | solution.py:13
  245.0 9.7 %collective-permute-start = (bf16[16,8192]{1,0:T(8,128)(2,1)}, bf16[16,8192]{1,0:T(8,128)(2,1)S(1)}, u32[]{:S(2)}, u32[]{:S(2)}) collective-permute-start(bf16[16,8192]{1,0:T(8,128)(2,1)} %add_convert_fusion.2), channel_id=1, source_target_pairs={{32,0},{64,32},{96,64},{128,96},{160,128},{192,160},{224,192},{256... | collective-permute-start | bytes 786440 | tf_op jit(solution)/shard_map/while/body/eval_jaxpr/ppermute | solution.py:13
  259.6 11.3 %collective-permute-start = (bf16[16,8192]{1,0:T(8,128)(2,1)}, bf16[16,8192]{1,0:T(8,128)(2,1)S(1)}, u32[]{:S(2)}, u32[]{:S(2)}) collective-permute-start(bf16[16,8192]{1,0:T(8,128)(2,1)} %add_convert_fusion.2), channel_id=1, source_target_pairs={{32,0},{64,32},{96,64},{128,96},{160,128},{192,160},{224,192},{256... | collective-permute-start | bytes 786440 | tf_op jit(solution)/shard_map/while/body/eval_jaxpr/ppermute | solution.py:13
  275.8 11.9 %collective-permute-start = (bf16[16,8192]{1,0:T(8,128)(2,1)}, bf16[16,8192]{1,0:T(8,128)(2,1)S(1)}, u32[]{:S(2)}, u32[]{:S(2)}) collective-permute-start(bf16[16,8192]{1,0:T(8,128)(2,1)} %add_convert_fusion.2), channel_id=1, source_target_pairs={{32,0},{64,32},{96,64},{128,96},{160,128},{192,160},{224,192},{256... | collective-permute-start | bytes 786440 | tf_op jit(solution)/shard_map/while/body/eval_jaxpr/ppermute | solution.py:13
  292.7 11.2 %collective-permute-start = (bf16[16,8192]{1,0:T(8,128)(2,1)}, bf16[16,8192]{1,0:T(8,128)(2,1)S(1)}, u32[]{:S(2)}, u32[]{:S(2)}) collective-permute-start(bf16[16,8192]{1,0:T(8,128)(2,1)} %add_convert_fusion.2), channel_id=1, source_target_pairs={{32,0},{64,32},{96,64},{128,96},{160,128},{192,160},{224,192},{256... | collective-permute-start | bytes 786440 | tf_op jit(solution)/shard_map/while/body/eval_jaxpr/ppermute | solution.py:13
  308.8 9.2 %collective-permute-start = (bf16[16,8192]{1,0:T(8,128)(2,1)}, bf16[16,8192]{1,0:T(8,128)(2,1)S(1)}, u32[]{:S(2)}, u32[]{:S(2)}) collective-permute-start(bf16[16,8192]{1,0:T(8,128)(2,1)} %add_convert_fusion.2), channel_id=1, source_target_pairs={{32,0},{64,32},{96,64},{128,96},{160,128},{192,160},{224,192},{256... | collective-permute-start | bytes 786440 | tf_op jit(solution)/shard_map/while/body/eval_jaxpr/ppermute | solution.py:13
  322.9 8.0 %collective-permute-start = (bf16[16,8192]{1,0:T(8,128)(2,1)}, bf16[16,8192]{1,0:T(8,128)(2,1)S(1)}, u32[]{:S(2)}, u32[]{:S(2)}) collective-permute-start(bf16[16,8192]{1,0:T(8,128)(2,1)} %add_convert_fusion.2), channel_id=1, source_target_pairs={{32,0},{64,32},{96,64},{128,96},{160,128},{192,160},{224,192},{256... | collective-permute-start | bytes 786440 | tf_op jit(solution)/shard_map/while/body/eval_jaxpr/ppermute | solution.py:13
  348.4 8.2 %collective-permute-start = (bf16[16,8192]{1,0:T(8,128)(2,1)}, bf16[16,8192]{1,0:T(8,128)(2,1)S(1)}, u32[]{:S(2)}, u32[]{:S(2)}) collective-permute-start(bf16[16,8192]{1,0:T(8,128)(2,1)} %add_convert_fusion.2), channel_id=1, source_target_pairs={{32,0},{64,32},{96,64},{128,96},{160,128},{192,160},{224,192},{256... | collective-permute-start | bytes 786440 | tf_op jit(solution)/shard_map/while/body/eval_jaxpr/ppermute | solution.py:13
  361.5 8.5 %collective-permute-start = (bf16[16,8192]{1,0:T(8,128)(2,1)}, bf16[16,8192]{1,0:T(8,128)(2,1)S(1)}, u32[]{:S(2)}, u32[]{:S(2)}) collective-permute-start(bf16[16,8192]{1,0:T(8,128)(2,1)} %add_convert_fusion.2), channel_id=1, source_target_pairs={{32,0},{64,32},{96,64},{128,96},{160,128},{192,160},{224,192},{256... | collective-permute-start | bytes 786440 | tf_op jit(solution)/shard_map/while/body/eval_jaxpr/ppermute | solution.py:13
  374.9 8.5 %collective-permute-start = (bf16[16,8192]{1,0:T(8,128)(2,1)}, bf16[16,8192]{1,0:T(8,128)(2,1)S(1)}, u32[]{:S(2)}, u32[]{:S(2)}) collective-permute-start(bf16[16,8192]{1,0:T(8,128)(2,1)} %add_convert_fusion.2), channel_id=1, source_target_pairs={{32,0},{64,32},{96,64},{128,96},{160,128},{192,160},{224,192},{256... | collective-permute-start | bytes 786440 | tf_op jit(solution)/shard_map/while/body/eval_jaxpr/ppermute | solution.py:13
  388.4 8.5 %collective-permute-start = (bf16[16,8192]{1,0:T(8,128)(2,1)}, bf16[16,8192]{1,0:T(8,128)(2,1)S(1)}, u32[]{:S(2)}, u32[]{:S(2)}) collective-permute-start(bf16[16,8192]{1,0:T(8,128)(2,1)} %add_convert_fusion.2), channel_id=1, source_target_pairs={{32,0},{64,32},{96,64},{128,96},{160,128},{192,160},{224,192},{256... | collective-permute-start | bytes 786440 | tf_op jit(solution)/shard_map/while/body/eval_jaxpr/ppermute | solution.py:13
  410.5 174.8 %all-gather.7.cloned.1.call-start = ((), (), s32[]{:S(2)}) async-start(), calls=%async_computation.3 | async-start | bytes 1474560 | tf_op jit(solution)/shard_map/all_gather | solution.py:97
  (10 other events, 31.0 us)
Sparse Core Ops, SparseCore 0:
  11.0 63.9 all-gather.4
  410.7 65.7 reduce-scatter.1
  478.6 31.4 all-gather.6
where the time goes:
time: 597 us; the launch traced here: 594 us
  waiting for transfers between devices  306 us (51%)
  blocking collectives  106 us (18%)
  other arithmetic  75.5 us (13%)
  matrix products  54.4 us (9%)
  starting transfers between devices  29.6 us (5%)
  between operations  13.9 us (2%)
  local copies, waits for them, and re-layouts  8.42 us (1%)
    ppermute x23, waiting for transfers between devices, from_behind(): lax.ppermute(value, axis, [(source, source + steps) for source in range(i...  176 us
    psum x1, blocking collectives, on_device(): totals = lax.psum(squares, ('pipe', 'seq', 'dp'))  106 us
    reduce_scatter x1, waiting for transfers between devices, on_device(): part = lax.psum_scatter(grads, 'seq', scatter_dimension=1, tiled=True)  65.9 us
    all_gather x1, waiting for transfers between devices, on_device(): whole = lax.all_gather(params, ('seq', 'dp'), axis=1, tiled=True)  64.3 us
    dot_general x23, matrix products, back_block(): jnp.dot(d_low, a_full, preferred_element_type=jnp.float32)  44.9 us
    convert_element_type x23, other arithmetic, back_block(): return hidden_gradient.astype(jnp.bfloat16)  42.7 us
    ppermute x23, starting transfers between devices, from_behind(): lax.ppermute(value, axis, [(source, source + steps) for source in range(i...  29.4 us
    dynamic_update_slice x23, other arithmetic, turn(): store = lax.dynamic_update_slice_in_dim(store, source[None], slot, 0)  23.3 us
  transfers between devices with their start and end apart: 26, of which 25 were waited for; matrix products, arithmetic and copies ran while one was open for 1% of the time, Pallas kernels for 0%

commit v1 on v0

--- a/solution.py
+++ b/solution.py
@@ -20,7 +20,8 @@
     top = top_grad[0]
     rank = a_rows.shape[1]
     params = jnp.concatenate([a_rows[0], b_rows[0], gain], axis=0)
-    whole = lax.all_gather(params, ("seq", "dp"), axis=1, tiled=True)
+    copies = jnp.concatenate([params] * lax.axis_size(("seq", "dp")), axis=1)
+    whole = lax.all_to_all(copies, ("seq", "dp"), 1, 1, tiled=True)
     a_full = whole[:rank]
     b_full = whole[rank : 2 * rank]
     gain_float = whole[2 * rank].astype(jnp.float32)

time: 597 us -> 570 us (0.955)
  waiting for transfers between devices: 306 us -> 260 us
  starting transfers between devices: 29.6 us -> 40.1 us
  other arithmetic: 75.5 us -> 84.4 us
    all_gather x1 -> x0, waiting for transfers between devices: 64.3 us -> none  [on_device(): whole = lax.all_gather(params, ('seq', 'dp'), axis=1, tiled=True)]
    all_to_all x0 -> x1, waiting for transfers between devices: none -> 16.8 us  [on_device(): whole = lax.all_to_all(copies, ('seq', 'dp'), 1, 1, tiled=True)]
    unnamed x0 -> x31, other arithmetic: none -> 13 us
    all_to_all x0 -> x1, starting transfers between devices: none -> 10.6 us  [on_device(): whole = lax.all_to_all(copies, ('seq', 'dp'), 1, 1, tiled=True)]
where the time goes in v1:
time: 570 us; the launch traced here: 566 us
  waiting for transfers between devices  260 us (46%)
  blocking collectives  106 us (19%)
  other arithmetic  84.4 us (15%)
  matrix products  50.8 us (9%)
  starting transfers between devices  40.1 us (7%)
  between operations  14.3 us (3%)
  local copies, waits for them, and re-layouts  9.5 us (2%)
    ppermute x23, waiting for transfers between devices, from_behind(): lax.ppermute(value, axis, [(source, source + steps) for source in range(i...  173 us
    psum x1, blocking collectives, on_device(): totals = lax.psum(squares, ('pipe', 'seq', 'dp'))  106 us
    reduce_scatter x1, waiting for transfers between devices, on_device(): part = lax.psum_scatter(grads, 'seq', scatter_dimension=1, tiled=True)  70.7 us
    dot_general x23, matrix products, back_block(): jnp.dot(d_low, a_full, preferred_element_type=jnp.float32)  44.9 us
    convert_element_type x23, other arithmetic, back_block(): return hidden_gradient.astype(jnp.bfloat16)  42.5 us
    ppermute x23, starting transfers between devices, from_behind(): lax.ppermute(value, axis, [(source, source + steps) for source in range(i...  29.4 us
    dynamic_update_slice x23, other arithmetic, turn(): store = lax.dynamic_update_slice_in_dim(store, source[None], slot, 0)  23.3 us
    all_to_all x1, waiting for transfers between devices, on_device(): whole = lax.all_to_all(copies, ('seq', 'dp'), 1, 1, tiled=True)  16.8 us
  transfers between devices with their start and end apart: 26, of which 25 were waited for; matrix products, arithmetic and copies ran while one was open for 1% of the time, Pallas kernels for 0%

profile of v1, /device:TPU:1, one launch (start us, length us, event | category | flops | bytes accessed | tf_op | source)
XLA Modules:
  0.0 566.1 jit_solution(4059780460185855338)
XLA Ops:
  22.3 10.6 %all-to-all-start = ((bf16[65,32,256]{2,0,1:T(8,128)(2,1)}), bf16[65,32,256]{2,0,1:T(8,128)(2,1)S(1)}, u32[]{:S(2)}, u32[]{:S(2)}) async-start(bf16[65,32,256]{2,0,1:T(8,128)(2,1)} %copy.9), calls=%async_computation | async-start | bytes 2359296 | tf_op jit(solution)/shard_map/all_to_all | solution.py:24
  33.5 16.8 %all-to-all-done = bf16[65,32,256]{2,0,1:T(8,128)(2,1)S(1)} async-done(((bf16[65,32,256]{2,0,1:T(8,128)(2,1)}), bf16[65,32,256]{2,0,1:T(8,128)(2,1)S(1)}, u32[]{:S(2)}, u32[]{:S(2)}) %all-to-all-start) | async-done | bytes 1064992 | tf_op jit(solution)/shard_map/all_to_all | solution.py:24
  52.4 315.4 %while.17 = (s32[]{:T(128)}, bf16[16,8192]{1,0:T(8,128)(2,1)S(1)}, bf16[9,16,8192]{2,1,0:T(8,128)(2,1)S(1)}, pred[]{:T(512)}, s32[]{:T(128)}, /*index=5*/bf16[12...) while((s32[]{:T(128)}, bf16[16,8192]{1,0:T(8,128)(2,1)S(1)}, ...), condition=%wide.region_3.4_spmd, body=%wide.region_1.3_spmd.sunk | while | flops 18612752 | bytes 5538680 | solution.py:78
  58.7 7.4 %collective-permute-done = bf16[16,8192]{1,0:T(8,128)(2,1)S(1)} collective-permute-done((bf16[16,8192]{1,0:T(8,128)(2,1)}, bf16[16,8192]{1,0:T(8,128)(2,1)S(1)}, u32[]{:S(2)}, u32[]{:S(2)}) %collective-permute-start) | collective-permute-done | bytes 262176 | tf_op jit(solution)/shard_map/while/body/eval_jaxpr/ppermute | solution.py:13
  97.2 7.2 %collective-permute-done = bf16[16,8192]{1,0:T(8,128)(2,1)S(1)} collective-permute-done((bf16[16,8192]{1,0:T(8,128)(2,1)}, bf16[16,8192]{1,0:T(8,128)(2,1)S(1)}, u32[]{:S(2)}, u32[]{:S(2)}) %collective-permute-start) | collective-permute-done | bytes 262176 | tf_op jit(solution)/shard_map/while/body/eval_jaxpr/ppermute | solution.py:13
  123.3 7.2 %collective-permute-done = bf16[16,8192]{1,0:T(8,128)(2,1)S(1)} collective-permute-done((bf16[16,8192]{1,0:T(8,128)(2,1)}, bf16[16,8192]{1,0:T(8,128)(2,1)S(1)}, u32[]{:S(2)}, u32[]{:S(2)}) %collective-permute-start) | collective-permute-done | bytes 262176 | tf_op jit(solution)/shard_map/while/body/eval_jaxpr/ppermute | solution.py:13
  136.7 7.2 %collective-permute-done = bf16[16,8192]{1,0:T(8,128)(2,1)S(1)} collective-permute-done((bf16[16,8192]{1,0:T(8,128)(2,1)}, bf16[16,8192]{1,0:T(8,128)(2,1)S(1)}, u32[]{:S(2)}, u32[]{:S(2)}) %collective-permute-start) | collective-permute-done | bytes 262176 | tf_op jit(solution)/shard_map/while/body/eval_jaxpr/ppermute | solution.py:13
  150.1 7.2 %collective-permute-done = bf16[16,8192]{1,0:T(8,128)(2,1)S(1)} collective-permute-done((bf16[16,8192]{1,0:T(8,128)(2,1)}, bf16[16,8192]{1,0:T(8,128)(2,1)S(1)}, u32[]{:S(2)}, u32[]{:S(2)}) %collective-permute-start) | collective-permute-done | bytes 262176 | tf_op jit(solution)/shard_map/while/body/eval_jaxpr/ppermute | solution.py:13
  163.5 7.2 %collective-permute-done = bf16[16,8192]{1,0:T(8,128)(2,1)S(1)} collective-permute-done((bf16[16,8192]{1,0:T(8,128)(2,1)}, bf16[16,8192]{1,0:T(8,128)(2,1)S(1)}, u32[]{:S(2)}, u32[]{:S(2)}) %collective-permute-start) | collective-permute-done | bytes 262176 | tf_op jit(solution)/shard_map/while/body/eval_jaxpr/ppermute | solution.py:13
  176.9 7.2 %collective-permute-done = bf16[16,8192]{1,0:T(8,128)(2,1)S(1)} collective-permute-done((bf16[16,8192]{1,0:T(8,128)(2,1)}, bf16[16,8192]{1,0:T(8,128)(2,1)S(1)}, u32[]{:S(2)}, u32[]{:S(2)}) %collective-permute-start) | collective-permute-done | bytes 262176 | tf_op jit(solution)/shard_map/while/body/eval_jaxpr/ppermute | solution.py:13
  190.4 7.2 %collective-permute-done = bf16[16,8192]{1,0:T(8,128)(2,1)S(1)} collective-permute-done((bf16[16,8192]{1,0:T(8,128)(2,1)}, bf16[16,8192]{1,0:T(8,128)(2,1)S(1)}, u32[]{:S(2)}, u32[]{:S(2)}) %collective-permute-start) | collective-permute-done | bytes 262176 | tf_op jit(solution)/shard_map/while/body/eval_jaxpr/ppermute | solution.py:13
  203.8 8.3 %collective-permute-done = bf16[16,8192]{1,0:T(8,128)(2,1)S(1)} collective-permute-done((bf16[16,8192]{1,0:T(8,128)(2,1)}, bf16[16,8192]{1,0:T(8,128)(2,1)S(1)}, u32[]{:S(2)}, u32[]{:S(2)}) %collective-permute-start) | collective-permute-done | bytes 262176 | tf_op jit(solution)/shard_map/while/body/eval_jaxpr/ppermute | solution.py:13
  218.3 9.9 %collective-permute-done = bf16[16,8192]{1,0:T(8,128)(2,1)S(1)} collective-permute-done((bf16[16,8192]{1,0:T(8,128)(2,1)}, bf16[16,8192]{1,0:T(8,128)(2,1)S(1)}, u32[]{:S(2)}, u32[]{:S(2)}) %collective-permute-start) | collective-permute-done | bytes 262176 | tf_op jit(solution)/shard_map/while/body/eval_jaxpr/ppermute | solution.py:13
  234.4 10.7 %collective-permute-done = bf16[16,8192]{1,0:T(8,128)(2,1)S(1)} collective-permute-done((bf16[16,8192]{1,0:T(8,128)(2,1)}, bf16[16,8192]{1,0:T(8,128)(2,1)S(1)}, u32[]{:S(2)}, u32[]{:S(2)}) %collective-permute-start) | collective-permute-done | bytes 262176 | tf_op jit(solution)/shard_map/while/body/eval_jaxpr/ppermute | solution.py:13
  251.3 9.8 %collective-permute-done = bf16[16,8192]{1,0:T(8,128)(2,1)S(1)} collective-permute-done((bf16[16,8192]{1,0:T(8,128)(2,1)}, bf16[16,8192]{1,0:T(8,128)(2,1)S(1)}, u32[]{:S(2)}, u32[]{:S(2)}) %collective-permute-start) | collective-permute-done | bytes 262176 | tf_op jit(solution)/shard_map/while/body/eval_jaxpr/ppermute | solution.py:13
  267.3 8.3 %collective-permute-done = bf16[16,8192]{1,0:T(8,128)(2,1)S(1)} collective-permute-done((bf16[16,8192]{1,0:T(8,128)(2,1)}, bf16[16,8192]{1,0:T(8,128)(2,1)S(1)}, u32[]{:S(2)}, u32[]{:S(2)}) %collective-permute-start) | collective-permute-done | bytes 262176 | tf_op jit(solution)/shard_map/while/body/eval_jaxpr/ppermute | solution.py:13
  281.7 6.7 %collective-permute-done = bf16[16,8192]{1,0:T(8,128)(2,1)S(1)} collective-permute-done((bf16[16,8192]{1,0:T(8,128)(2,1)}, bf16[16,8192]{1,0:T(8,128)(2,1)S(1)}, u32[]{:S(2)}, u32[]{:S(2)}) %collective-permute-start) | collective-permute-done | bytes 262176 | tf_op jit(solution)/shard_map/while/body/eval_jaxpr/ppermute | solution.py:13
  307.2 7.0 %collective-permute-done = bf16[16,8192]{1,0:T(8,128)(2,1)S(1)} collective-permute-done((bf16[16,8192]{1,0:T(8,128)(2,1)}, bf16[16,8192]{1,0:T(8,128)(2,1)S(1)}, u32[]{:S(2)}, u32[]{:S(2)}) %collective-permute-start) | collective-permute-done | bytes 262176 | tf_op jit(solution)/shard_map/while/body/eval_jaxpr/ppermute | solution.py:13
  320.3 7.2 %collective-permute-done = bf16[16,8192]{1,0:T(8,128)(2,1)S(1)} collective-permute-done((bf16[16,8192]{1,0:T(8,128)(2,1)}, bf16[16,8192]{1,0:T(8,128)(2,1)S(1)}, u32[]{:S(2)}, u32[]{:S(2)}) %collective-permute-start) | collective-permute-done | bytes 262176 | tf_op jit(solution)/shard_map/while/body/eval_jaxpr/ppermute | solution.py:13
  333.7 7.2 %collective-permute-done = bf16[16,8192]{1,0:T(8,128)(2,1)S(1)} collective-permute-done((bf16[16,8192]{1,0:T(8,128)(2,1)}, bf16[16,8192]{1,0:T(8,128)(2,1)S(1)}, u32[]{:S(2)}, u32[]{:S(2)}) %collective-permute-start) | collective-permute-done | bytes 262176 | tf_op jit(solution)/shard_map/while/body/eval_jaxpr/ppermute | solution.py:13
  347.1 7.2 %collective-permute-done = bf16[16,8192]{1,0:T(8,128)(2,1)S(1)} collective-permute-done((bf16[16,8192]{1,0:T(8,128)(2,1)}, bf16[16,8192]{1,0:T(8,128)(2,1)S(1)}, u32[]{:S(2)}, u32[]{:S(2)}) %collective-permute-start) | collective-permute-done | bytes 262176 | tf_op jit(solution)/shard_map/while/body/eval_jaxpr/ppermute | solution.py:13
  360.6 7.2 %collective-permute-done = bf16[16,8192]{1,0:T(8,128)(2,1)S(1)} collective-permute-done((bf16[16,8192]{1,0:T(8,128)(2,1)}, bf16[16,8192]{1,0:T(8,128)(2,1)S(1)}, u32[]{:S(2)}, u32[]{:S(2)}) %collective-permute-start) | collective-permute-done | bytes 262176 | tf_op jit(solution)/shard_map/while/body/eval_jaxpr/ppermute | solution.py:13
  377.4 70.7 %reduce-scatter.2.cloned.1.call-done = f32[65,1024]{1,0:T(8,128)} async-done(((f32[65,8192]{1,0:T(8,128)}), f32[65,1024]{1,0:T(8,128)}) %reduce-scatter.2.cloned.1.call-update) | async-done | bytes 266256 | tf_op jit(solution)/shard_map/reduce_scatter | solution.py:90
  450.4 106.0 %psum.7 = f32[4]{0:T(128)S(1)} all-reduce(f32[4]{0:T(128)S(1)} %compare_select_fusion), channel_id=1, replica_groups=mesh['pipe'=16,'seq'=8,'dp'=4] {'pipe','seq','dp'}, use_global_device_ids=true, to_apply=%region_7.8 | all-reduce | flops 4 | bytes 32 | tf_op jit(solution)/shard_map/psum | solution.py:95
  (219 shorter events, 199.7 us)
Async XLA Ops:
  22.3 28.0 %all-to-all-start = ((bf16[65,32,256]{2,0,1:T(8,128)(2,1)}), bf16[65,32,256]{2,0,1:T(8,128)(2,1)S(1)}, u32[]{:S(2)}, u32[]{:S(2)}) async-start(bf16[65,32,256]{2,0,1:T(8,128)(2,1)} %copy.9), calls=%async_computation | async-start | bytes 2359296 | tf_op jit(solution)/shard_map/all_to_all | solution.py:24
  32.9 415.2 %reduce-scatter.2.cloned.1.call-start = ((), (), s32[]{:S(2)}) async-start(), calls=%async_computation.2 | async-start | bytes 2654208 | tf_op jit(solution)/shard_map/reduce_scatter | solution.py:90
  57.4 8.7 %collective-permute-start = (bf16[16,8192]{1,0:T(8,128)(2,1)}, bf16[16,8192]{1,0:T(8,128)(2,1)S(1)}, u32[]{:S(2)}, u32[]{:S(2)}) collective-permute-start(bf16[16,8192]{1,0:T(8,128)(2,1)} %add_convert_fusion.2), channel_id=1, source_target_pairs={{32,0},{64,32},{96,64},{128,96},{160,128},{192,160},{224,192},{256... | collective-permute-start | bytes 786440 | tf_op jit(solution)/shard_map/while/body/eval_jaxpr/ppermute | solution.py:13
  70.9 7.8 %collective-permute-start = (bf16[16,8192]{1,0:T(8,128)(2,1)}, bf16[16,8192]{1,0:T(8,128)(2,1)S(1)}, u32[]{:S(2)}, u32[]{:S(2)}) collective-permute-start(bf16[16,8192]{1,0:T(8,128)(2,1)} %add_convert_fusion.2), channel_id=1, source_target_pairs={{32,0},{64,32},{96,64},{128,96},{160,128},{192,160},{224,192},{256... | collective-permute-start | bytes 786440 | tf_op jit(solution)/shard_map/while/body/eval_jaxpr/ppermute | solution.py:13
  95.9 8.5 %collective-permute-start = (bf16[16,8192]{1,0:T(8,128)(2,1)}, bf16[16,8192]{1,0:T(8,128)(2,1)S(1)}, u32[]{:S(2)}, u32[]{:S(2)}) collective-permute-start(bf16[16,8192]{1,0:T(8,128)(2,1)} %add_convert_fusion.2), channel_id=1, source_target_pairs={{32,0},{64,32},{96,64},{128,96},{160,128},{192,160},{224,192},{256... | collective-permute-start | bytes 786440 | tf_op jit(solution)/shard_map/while/body/eval_jaxpr/ppermute | solution.py:13
  109.2 7.8 %collective-permute-start = (bf16[16,8192]{1,0:T(8,128)(2,1)}, bf16[16,8192]{1,0:T(8,128)(2,1)S(1)}, u32[]{:S(2)}, u32[]{:S(2)}) collective-permute-start(bf16[16,8192]{1,0:T(8,128)(2,1)} %add_convert_fusion.2), channel_id=1, source_target_pairs={{32,0},{64,32},{96,64},{128,96},{160,128},{192,160},{224,192},{256... | collective-permute-start | bytes 786440 | tf_op jit(solution)/shard_map/while/body/eval_jaxpr/ppermute | solution.py:13
  122.0 8.5 %collective-permute-start = (bf16[16,8192]{1,0:T(8,128)(2,1)}, bf16[16,8192]{1,0:T(8,128)(2,1)S(1)}, u32[]{:S(2)}, u32[]{:S(2)}) collective-permute-start(bf16[16,8192]{1,0:T(8,128)(2,1)} %add_convert_fusion.2), channel_id=1, source_target_pairs={{32,0},{64,32},{96,64},{128,96},{160,128},{192,160},{224,192},{256... | collective-permute-start | bytes 786440 | tf_op jit(solution)/shard_map/while/body/eval_jaxpr/ppermute | solution.py:13
  135.4 8.5 %collective-permute-start = (bf16[16,8192]{1,0:T(8,128)(2,1)}, bf16[16,8192]{1,0:T(8,128)(2,1)S(1)}, u32[]{:S(2)}, u32[]{:S(2)}) collective-permute-start(bf16[16,8192]{1,0:T(8,128)(2,1)} %add_convert_fusion.2), channel_id=1, source_target_pairs={{32,0},{64,32},{96,64},{128,96},{160,128},{192,160},{224,192},{256... | collective-permute-start | bytes 786440 | tf_op jit(solution)/shard_map/while/body/eval_jaxpr/ppermute | solution.py:13
  148.8 8.5 %collective-permute-start = (bf16[16,8192]{1,0:T(8,128)(2,1)}, bf16[16,8192]{1,0:T(8,128)(2,1)S(1)}, u32[]{:S(2)}, u32[]{:S(2)}) collective-permute-start(bf16[16,8192]{1,0:T(8,128)(2,1)} %add_convert_fusion.2), channel_id=1, source_target_pairs={{32,0},{64,32},{96,64},{128,96},{160,128},{192,160},{224,192},{256... | collective-permute-start | bytes 786440 | tf_op jit(solution)/shard_map/while/body/eval_jaxpr/ppermute | solution.py:13
  162.2 8.5 %collective-permute-start = (bf16[16,8192]{1,0:T(8,128)(2,1)}, bf16[16,8192]{1,0:T(8,128)(2,1)S(1)}, u32[]{:S(2)}, u32[]{:S(2)}) collective-permute-start(bf16[16,8192]{1,0:T(8,128)(2,1)} %add_convert_fusion.2), channel_id=1, source_target_pairs={{32,0},{64,32},{96,64},{128,96},{160,128},{192,160},{224,192},{256... | collective-permute-start | bytes 786440 | tf_op jit(solution)/shard_map/while/body/eval_jaxpr/ppermute | solution.py:13
  175.7 8.5 %collective-permute-start = (bf16[16,8192]{1,0:T(8,128)(2,1)}, bf16[16,8192]{1,0:T(8,128)(2,1)S(1)}, u32[]{:S(2)}, u32[]{:S(2)}) collective-permute-start(bf16[16,8192]{1,0:T(8,128)(2,1)} %add_convert_fusion.2), channel_id=1, source_target_pairs={{32,0},{64,32},{96,64},{128,96},{160,128},{192,160},{224,192},{256... | collective-permute-start | bytes 786440 | tf_op jit(solution)/shard_map/while/body/eval_jaxpr/ppermute | solution.py:13
  189.1 8.5 %collective-permute-start = (bf16[16,8192]{1,0:T(8,128)(2,1)}, bf16[16,8192]{1,0:T(8,128)(2,1)S(1)}, u32[]{:S(2)}, u32[]{:S(2)}) collective-permute-start(bf16[16,8192]{1,0:T(8,128)(2,1)} %add_convert_fusion.2), channel_id=1, source_target_pairs={{32,0},{64,32},{96,64},{128,96},{160,128},{192,160},{224,192},{256... | collective-permute-start | bytes 786440 | tf_op jit(solution)/shard_map/while/body/eval_jaxpr/ppermute | solution.py:13
  202.5 9.6 %collective-permute-start = (bf16[16,8192]{1,0:T(8,128)(2,1)}, bf16[16,8192]{1,0:T(8,128)(2,1)S(1)}, u32[]{:S(2)}, u32[]{:S(2)}) collective-permute-start(bf16[16,8192]{1,0:T(8,128)(2,1)} %add_convert_fusion.2), channel_id=1, source_target_pairs={{32,0},{64,32},{96,64},{128,96},{160,128},{192,160},{224,192},{256... | collective-permute-start | bytes 786440 | tf_op jit(solution)/shard_map/while/body/eval_jaxpr/ppermute | solution.py:13
  217.0 11.2 %collective-permute-start = (bf16[16,8192]{1,0:T(8,128)(2,1)}, bf16[16,8192]{1,0:T(8,128)(2,1)S(1)}, u32[]{:S(2)}, u32[]{:S(2)}) collective-permute-start(bf16[16,8192]{1,0:T(8,128)(2,1)} %add_convert_fusion.2), channel_id=1, source_target_pairs={{32,0},{64,32},{96,64},{128,96},{160,128},{192,160},{224,192},{256... | collective-permute-start | bytes 786440 | tf_op jit(solution)/shard_map/while/body/eval_jaxpr/ppermute | solution.py:13
  233.1 12.0 %collective-permute-start = (bf16[16,8192]{1,0:T(8,128)(2,1)}, bf16[16,8192]{1,0:T(8,128)(2,1)S(1)}, u32[]{:S(2)}, u32[]{:S(2)}) collective-permute-start(bf16[16,8192]{1,0:T(8,128)(2,1)} %add_convert_fusion.2), channel_id=1, source_target_pairs={{32,0},{64,32},{96,64},{128,96},{160,128},{192,160},{224,192},{256... | collective-permute-start | bytes 786440 | tf_op jit(solution)/shard_map/while/body/eval_jaxpr/ppermute | solution.py:13
  250.0 11.1 %collective-permute-start = (bf16[16,8192]{1,0:T(8,128)(2,1)}, bf16[16,8192]{1,0:T(8,128)(2,1)S(1)}, u32[]{:S(2)}, u32[]{:S(2)}) collective-permute-start(bf16[16,8192]{1,0:T(8,128)(2,1)} %add_convert_fusion.2), channel_id=1, source_target_pairs={{32,0},{64,32},{96,64},{128,96},{160,128},{192,160},{224,192},{256... | collective-permute-start | bytes 786440 | tf_op jit(solution)/shard_map/while/body/eval_jaxpr/ppermute | solution.py:13
  266.0 9.5 %collective-permute-start = (bf16[16,8192]{1,0:T(8,128)(2,1)}, bf16[16,8192]{1,0:T(8,128)(2,1)S(1)}, u32[]{:S(2)}, u32[]{:S(2)}) collective-permute-start(bf16[16,8192]{1,0:T(8,128)(2,1)} %add_convert_fusion.2), channel_id=1, source_target_pairs={{32,0},{64,32},{96,64},{128,96},{160,128},{192,160},{224,192},{256... | collective-permute-start | bytes 786440 | tf_op jit(solution)/shard_map/while/body/eval_jaxpr/ppermute | solution.py:13
  280.4 8.0 %collective-permute-start = (bf16[16,8192]{1,0:T(8,128)(2,1)}, bf16[16,8192]{1,0:T(8,128)(2,1)S(1)}, u32[]{:S(2)}, u32[]{:S(2)}) collective-permute-start(bf16[16,8192]{1,0:T(8,128)(2,1)} %add_convert_fusion.2), channel_id=1, source_target_pairs={{32,0},{64,32},{96,64},{128,96},{160,128},{192,160},{224,192},{256... | collective-permute-start | bytes 786440 | tf_op jit(solution)/shard_map/while/body/eval_jaxpr/ppermute | solution.py:13
  305.9 8.2 %collective-permute-start = (bf16[16,8192]{1,0:T(8,128)(2,1)}, bf16[16,8192]{1,0:T(8,128)(2,1)S(1)}, u32[]{:S(2)}, u32[]{:S(2)}) collective-permute-start(bf16[16,8192]{1,0:T(8,128)(2,1)} %add_convert_fusion.2), channel_id=1, source_target_pairs={{32,0},{64,32},{96,64},{128,96},{160,128},{192,160},{224,192},{256... | collective-permute-start | bytes 786440 | tf_op jit(solution)/shard_map/while/body/eval_jaxpr/ppermute | solution.py:13
  319.0 8.5 %collective-permute-start = (bf16[16,8192]{1,0:T(8,128)(2,1)}, bf16[16,8192]{1,0:T(8,128)(2,1)S(1)}, u32[]{:S(2)}, u32[]{:S(2)}) collective-permute-start(bf16[16,8192]{1,0:T(8,128)(2,1)} %add_convert_fusion.2), channel_id=1, source_target_pairs={{32,0},{64,32},{96,64},{128,96},{160,128},{192,160},{224,192},{256... | collective-permute-start | bytes 786440 | tf_op jit(solution)/shard_map/while/body/eval_jaxpr/ppermute | solution.py:13
  332.4 8.5 %collective-permute-start = (bf16[16,8192]{1,0:T(8,128)(2,1)}, bf16[16,8192]{1,0:T(8,128)(2,1)S(1)}, u32[]{:S(2)}, u32[]{:S(2)}) collective-permute-start(bf16[16,8192]{1,0:T(8,128)(2,1)} %add_convert_fusion.2), channel_id=1, source_target_pairs={{32,0},{64,32},{96,64},{128,96},{160,128},{192,160},{224,192},{256... | collective-permute-start | bytes 786440 | tf_op jit(solution)/shard_map/while/body/eval_jaxpr/ppermute | solution.py:13
  345.9 8.5 %collective-permute-start = (bf16[16,8192]{1,0:T(8,128)(2,1)}, bf16[16,8192]{1,0:T(8,128)(2,1)S(1)}, u32[]{:S(2)}, u32[]{:S(2)}) collective-permute-start(bf16[16,8192]{1,0:T(8,128)(2,1)} %add_convert_fusion.2), channel_id=1, source_target_pairs={{32,0},{64,32},{96,64},{128,96},{160,128},{192,160},{224,192},{256... | collective-permute-start | bytes 786440 | tf_op jit(solution)/shard_map/while/body/eval_jaxpr/ppermute | solution.py:13
  359.3 8.5 %collective-permute-start = (bf16[16,8192]{1,0:T(8,128)(2,1)}, bf16[16,8192]{1,0:T(8,128)(2,1)S(1)}, u32[]{:S(2)}, u32[]{:S(2)}) collective-permute-start(bf16[16,8192]{1,0:T(8,128)(2,1)} %add_convert_fusion.2), channel_id=1, source_target_pairs={{32,0},{64,32},{96,64},{128,96},{160,128},{192,160},{224,192},{256... | collective-permute-start | bytes 786440 | tf_op jit(solution)/shard_map/while/body/eval_jaxpr/ppermute | solution.py:13
  377.4 179.6 %all-gather.4.cloned.1.call-start = ((), (), s32[]{:S(2)}) async-start(), calls=%async_computation.3 | async-start | bytes 1474560 | tf_op jit(solution)/shard_map/all_gather | solution.py:98
  (10 other events, 69.7 us)
Sparse Core Ops, SparseCore 0:
  377.5 70.5 reduce-scatter.1
  450.2 31.4 all-gather.3
